TPU v7x, 128 devices: a whole 4x4x4 slice. The times are simulated.
128 devices in a mesh: seq: 4 (over x), exp: 32 (over y, z, core).
Axes of the slice: x: 4, y: 4, z: 4, core: 2. Of those that a mesh axis runs over, the one named last changes fastest.
Arguments:
- resid: bfloat16 [32, 384, 2048], P('exp', 'seq'), may hold values from -6 to 6
- qkv: bfloat16 [32, 384, 6144], P('exp', 'seq'), may hold values from -8 to 8
- w_out: bfloat16 [2048, 2048], P('seq'), may hold values from -0.125 to 0.125
- norm_gain: float32 [2048], replicated, may hold values from 0.1 to 1.9
- router_w: bfloat16 [2048, 64], replicated, may hold values from -0.125 to 0.125
- expert_ids: int32 [32, 384, 6], P('exp'), may hold values from 0 to 63, all different within a row; in each aligned block of 96 rows (0 to 95, 96 to 191, ..., all dimensions but the last counted through in order) at most 12 rows name the same one
- w_gate_up: bfloat16 [64, 2048, 2, 1408], P('exp', None, None, 'seq'), may hold values from -0.125 to 0.125
- w_down: bfloat16 [64, 1408, 2048], P('exp', 'seq'), may hold values from -0.15625 to 0.15625
Outputs:
- layer_out: bfloat16 [32, 384, 2048], P('exp', 'seq')
Inputs may be any that keep to these rules, and one draw needn't show every extreme that they name: `expert_ids`: each point names 6 different experts. In each aligned block of 96 points (the points of one device, in the order of sets and then points), no expert is named by more than 12 points, and in every draw some expert is named by exactly 12 points of some block.
All inputs are finite; a program needn't handle non-finite values.
Results may differ from a plain program's by a relative error of at most 0.0065.
Values may be sent and summed in bfloat16 or wider, within the bound.
No kernel may reach another device: no remote copies, remote signals or barrier semaphores. Data moves between devices by JAX's collectives and lax.ppermute only.
A program may use at most 128 MiB of HBM per device.

v0:
```python
import math
import jax
import jax.numpy as jnp
from jax import lax
from jax.sharding import PartitionSpec as P

H = 16
HD = 128
EXPERTS = 64
epsilon = 1e-05


def gate_weights(normed_rows, router_w, chosen):
    logits = jnp.dot(normed_rows, router_w, preferred_element_type=jnp.float32)
    match = chosen[:, :, None] == jnp.arange(logits.shape[1], dtype=jnp.int32)[None, None, :]
    picked = jnp.sum(jnp.where(match, logits[:, None, :], jnp.zeros((), logits.dtype)), axis=-1)
    squashed = jax.nn.sigmoid(picked)
    return squashed / jnp.sum(squashed, axis=-1, keepdims=True)


def slot_ranks(chosen, block_rows, experts):
    blocks = chosen.shape[0] // block_rows
    width = block_rows * chosen.shape[1]
    grouped = chosen.reshape(blocks, width)
    hits = (grouped[:, :, None] == jnp.arange(experts, dtype=jnp.int32)[None, None, :]).astype(
        jnp.bfloat16
    )
    lower = jnp.arange(width)[:, None] >= jnp.arange(width)[None, :]
    counts = jnp.einsum(
        "ij,bje->bie", lower.astype(jnp.bfloat16), hits, preferred_element_type=jnp.float32
    )
    ranks = jnp.sum(counts * hits.astype(jnp.float32), axis=-1) - 1
    return ranks.astype(jnp.int32).reshape(chosen.shape)


def expert_part(received, w_gate_up, w_down):
    both = jnp.einsum("aend,edgf->aengf", received, w_gate_up, preferred_element_type=jnp.float32)
    hidden = (jax.nn.silu(both[:, :, :, 0]) * both[:, :, :, 1]).astype(jnp.bfloat16)
    return jnp.einsum("aenf,efd->aend", hidden, w_down, preferred_element_type=jnp.float32)


def scatter_rows(normed_rows, slot_index, buffer_rows):
    slots = jnp.arange(buffer_rows, dtype=jnp.int32)
    select = jnp.sum((slot_index[None, :, :] == slots[:, None, None]).astype(jnp.bfloat16), axis=-1)
    return jnp.dot(select, normed_rows, preferred_element_type=jnp.float32).astype(jnp.bfloat16)


def combine_rows(out_table, slot_index, gate_vals):
    slots = jnp.arange(out_table.shape[0], dtype=jnp.int32)
    weights = jnp.sum(
        jnp.where(slot_index[:, :, None] == slots[None, None, :], gate_vals[:, :, None], 0.0),
        axis=1,
    )
    high = weights.astype(jnp.bfloat16)
    low = (weights - high.astype(jnp.float32)).astype(jnp.bfloat16)
    return jnp.dot(high, out_table, preferred_element_type=jnp.float32) + jnp.dot(
        low, out_table, preferred_element_type=jnp.float32
    )


def on_device(resid, qkv, w_out, norm_gain, router_w, expert_ids, w_gate_up, w_down):
    row_count = resid.shape[1]
    model_width = resid.shape[2]
    seq_size = lax.axis_size("seq")
    exp_size = lax.axis_size("exp")
    seq_length = row_count * seq_size
    head_local = H // seq_size
    local_width = head_local * HD
    packed = qkv.reshape(row_count, 3, seq_size, local_width)
    regrouped = lax.all_to_all(packed, "seq", split_axis=2, concat_axis=0, tiled=True)
    queries = regrouped[:, 0, 0].reshape(seq_length, head_local, HD)
    keys_all = regrouped[:, 1, 0].reshape(seq_length, head_local, HD)
    values_all = regrouped[:, 2, 0].reshape(seq_length, head_local, HD)
    query_block = min(seq_length, 512)

    def attend_block(query_rows):
        scores = jnp.einsum(
            "qhd,khd->hqk", query_rows, keys_all, preferred_element_type=jnp.float32
        ) / math.sqrt(HD)
        weights = jax.nn.softmax(scores, axis=-1).astype(jnp.bfloat16)
        mixed_heads = jnp.einsum(
            "hqk,khd->qhd", weights, values_all, preferred_element_type=jnp.float32
        )
        return mixed_heads.reshape(query_rows.shape[0], local_width).astype(jnp.bfloat16)

    attended = lax.map(
        attend_block, queries.reshape(seq_length // query_block, query_block, head_local, HD)
    )
    attended = attended.reshape(seq_length, local_width)
    back = lax.all_to_all(
        attended.reshape(seq_length, 1, local_width), "seq", split_axis=0, concat_axis=1, tiled=True
    )
    point_rows = back.reshape(row_count, model_width)
    projected = jnp.dot(
        point_rows,
        lax.all_gather(w_out, "seq", axis=0, tiled=True),
        preferred_element_type=jnp.float32,
    )
    mixed = resid[0].astype(jnp.float32) + projected
    meansq = jnp.mean(mixed * mixed, axis=-1, keepdims=True)
    normed = (mixed * lax.rsqrt(meansq + epsilon) * norm_gain).astype(jnp.bfloat16)
    exp_local = w_gate_up.shape[0]
    slot_cap = row_count // 8
    gathered = lax.all_gather(normed, "seq", axis=0, tiled=True)
    chosen = expert_ids[0]
    gate_vals = gate_weights(gathered, router_w, chosen)
    ranks = slot_ranks(chosen, row_count, EXPERTS)
    owner_rows = seq_size * slot_cap
    source_block = (jnp.arange(seq_length, dtype=jnp.int32) // row_count)[:, None]
    slot_index = chosen * owner_rows + source_block * slot_cap + ranks
    outgoing = scatter_rows(gathered, slot_index, EXPERTS * owner_rows)
    outgoing = outgoing.reshape(exp_size, exp_local, owner_rows, model_width)
    partial_out = expert_part(
        lax.all_to_all(outgoing, "exp", split_axis=0, concat_axis=0, tiled=True), w_gate_up, w_down
    ).astype(jnp.bfloat16)
    returned = lax.all_to_all(partial_out, "exp", split_axis=0, concat_axis=0, tiled=True)
    out_table = returned.reshape(-1, model_width)
    expert_sum = lax.psum_scatter(
        combine_rows(out_table, slot_index, gate_vals).astype(jnp.bfloat16),
        "seq",
        scatter_dimension=0,
        tiled=True,
    ).astype(jnp.float32)
    return (mixed + expert_sum).astype(jnp.bfloat16).reshape(1, row_count, model_width)


def solution(mesh):
    in_specs = (
        P("exp", "seq", None),
        P("exp", "seq", None),
        P("seq", None),
        P(),
        P(),
        P("exp", None, None),
        P("exp", None, None, "seq"),
        P("exp", "seq", None),
    )
    out_specs = P("exp", "seq", None)
    return jax.shard_map(
        on_device, mesh=mesh, in_specs=in_specs, out_specs=out_specs, check_vma=False
    )
```

profile of v0, /device:TPU:0, one launch (start us, length us, event | category | flops | bytes accessed | tf_op | source)
XLA Modules:
  0.0 582.8 jit_solution(9345225432618470734)
XLA Ops:
  7.3 2.9 reshape.139
  11.7 27.4 %all_to_all.43 = bf16[96,3,4,512]{3,0,1,2:T(8,128)(2,1)S(1)} all-to-all(bf16[96,3,4,512]{3,0,1,2:T(8,128)(2,1)S(1)} %copy.111), channel_id=1, replica_groups=mesh['seq'=4,'exp'=32] {'seq'}, dimensions={2} | all-to-all | bytes 2359296 | tf_op jit(solution)/shard_map/all_to_all | solution.py:70
  40.2 1.9 copy.117
  42.2 1.9 copy.113
  45.0 3.5 fusion.49
  48.5 2.2 convolution_convert_fusion.1
  54.9 15.5 %all_to_all.44 = bf16[4,2,24576]{2,1,0:T(2,128)(2,1)S(1)} all-to-all(bf16[4,2,24576]{2,1,0:T(2,128)(2,1)} %reshape.149), channel_id=1, replica_groups=mesh['seq'=4,'exp'=32] {'seq'}, dimensions={0} | all-to-all | bytes 786432 | tf_op jit(solution)/shard_map/all_to_all | solution.py:90
  70.4 1.7 reshape.150
  73.7 30.5 %all-gather.3.cloned.1.call-done = bf16[2048,2048]{1,0:T(8,128)(2,1)} async-done(((bf16[512,2048]{1,0:T(8,128)(2,1)}), bf16[2048,2048]{1,0:T(8,128)(2,1)}) %all-gather.3.cloned.1.call-update) | async-done | bytes 8388624 | tf_op jit(solution)/shard_map/all_gather | solution.py:96
  104.1 5.0 multiply_reduce_fusion.1
  112.2 5.6 fusion.2
  117.8 20.6 %all-gather.5.cloned.1.call-done = bf16[384,2048]{1,0:T(8,128)(2,1)} async-done(((bf16[96,2048]{1,0:T(8,128)(2,1)}), bf16[384,2048]{1,0:T(8,128)(2,1)}) %all-gather.5.cloned.1.call-update) | async-done | bytes 1572880 | tf_op jit(solution)/shard_map/all_gather | solution.py:104
  138.4 8.7 %convolution_convert_fusion = bf16[3072,2048]{1,0:T(8,128)(2,1)S(1)} fusion(bf16[3072,384]{1,0:T(8,128)(2,1)} %fusion.2, bf16[384,2048]{1,0:T(8,128)(2,1)} %all-gather.5.cloned.1.call-done), kind=kOutput, calls=%fused_computation.9 | convolution fusion | flops 4838129664 | bytes 16515072 | tf_op jit(solution)/shard_map/dot_general | solution.py:45
  147.1 147.5 %all_to_all.45 = bf16[32,2,48,2048]{3,2,1,0:T(8,128)(2,1)} all-to-all(bf16[32,2,48,2048]{3,2,1,0:T(8,128)(2,1)S(1)} %bitcast.99), channel_id=1, replica_groups=mesh['seq'=4,'exp'=32] {'exp'}, dimensions={0} | all-to-all | bytes 25165824 | tf_op jit(solution)/shard_map/all_to_all | solution.py:114
  294.6 16.0 %fusion.8 = f32[32,2,48,2,352]{4,2,3,0,1:T(8,128)} fusion(bf16[2,2048,2,352]{1,3,2,0:T(8,128)(2,1)} %param.14, bf16[32,2,48,2048]{3,2,1,0:T(8,128)(2,1)} %all_to_all.45), kind=kOutput, calls=%fused_computation.16 | convolution fusion | flops 8858370048 | bytes 27000832 | tf_op jit(solution)/shard_map/aend,edgf->aengf/dot_general | solution.py:37
  310.6 10.7 %convert_bitcast_fusion = bf16[32,2,48,2048]{3,2,0,1:T(8,128)(2,1)S(1)} fusion(bf16[2,352,2048]{2,1,0:T(8,128)(2,1)S(1)} %copy-done, f32[32,2,48,2,352]{4,2,3,0,1:T(8,128)} %fusion.8), kind=kOutput, calls=%fused_computation.8 | convolution fusion | flops 4441964544 | bytes 24117248 | tf_op jit(solution)/shard_map/aenf,efd->aend/dot_general | solution.py:39
  321.3 5.2 copy.128
  326.5 5.2 all-to-all-start.3
  333.2 8.6 %select_reduce_fusion = f32[384,3072]{1,0:T(8,128)} fusion(f32[384,6]{0,1:T(8,128)S(1)} %multiply_divide_fusion, s32[384,6]{0,1:T(8,128)S(1)} %copy.123), kind=kLoop, calls=%fused_computation.2 | loop fusion | flops 20054016 | bytes 4737024 | tf_op jit(solution)/shard_map/reduce_sum | solution.py:50
  341.7 167.1 %all-to-all-done.3 = bf16[32,2,48,2048]{3,2,1,0:T(8,128)(2,1)} async-done(((bf16[32,2,48,2048]{3,2,1,0:T(8,128)(2,1)}), bf16[32,2,48,2048]{3,2,1,0:T(8,128)(2,1)}, u32[]{:S(2)}, u32[]{:S(2)}) %all-to-all-start.3) | async-done | bytes 12582944 | tf_op jit(solution)/shard_map/all_to_all | solution.py:116
  508.9 11.0 %fusion.32 = f32[384,2048]{1,0:T(8,128)S(1)} fusion(bf16[3072,2048]{1,0:T(8,128)(2,1)} %bitcast.26, f32[384,3072]{1,0:T(8,128)} %select_reduce_fusion), kind=kOutput, calls=%fused_computation.33 | convolution fusion | flops 4833017856 | bytes 20447232 | tf_op jit(solution)/shard_map/dot_general | solution.py:56
  519.9 9.8 %add_convert_fusion = bf16[384,2048]{1,0:T(8,128)(2,1)} fusion(f32[384,2048]{1,0:T(8,128)S(1)} %fusion.32, bf16[3072,2048]{1,0:T(8,128)(2,1)} %bitcast.26, f32[384,3072]{1,0:T(8,128)S(1)} %copy-done.3), kind=kOutput, calls=%fused_computation.17 | convolution fusion | flops 4838129664 | bytes 22020096 | tf_op jit(solution)/shard_map/dot_general | solution.py:56
  529.7 44.4 %reduce-scatter.2.cloned.1.call-done = bf16[96,2048]{1,0:T(8,128)(2,1)} async-done(((bf16[384,2048]{1,0:T(8,128)(2,1)}), bf16[96,2048]{1,0:T(8,128)(2,1)}) %reduce-scatter.2.cloned.1.call-update) | async-done | bytes 393232 | tf_op jit(solution)/shard_map/reduce_scatter | solution.py:118
  574.2 2.1 fusion.36
  (52 shorter events, 14.5 us)
Async XLA Ops:
  6.5 304.1 %copy-start = (bf16[2,352,2048]{2,1,0:T(8,128)(2,1)S(1)}, bf16[2,352,2048]{2,1,0:T(8,128)(2,1)}, u32[]{:S(2)}) copy-start(bf16[2,352,2048]{2,1,0:T(8,128)(2,1)} %param.15) | copy-start | bytes 8650756
  6.5 97.6 %all-gather.3.cloned.1.call-start = ((), (), s32[]{:S(2)}) async-start(), calls=%async_computation.5 | async-start | bytes 10485760 | tf_op jit(solution)/shard_map/all_gather | solution.py:96
  7.3 131.1 %all-gather.5.cloned.1.call-start = ((), (), s32[]{:S(2)}) async-start(), calls=%async_computation.6 | async-start | bytes 1966080 | tf_op jit(solution)/shard_map/all_gather | solution.py:104
  104.1 6.0 %copy-start.7 = (f32[2048]{0:T(1024)S(1)}, f32[2048]{0:T(1024)}, u32[]{:S(2)}) copy-start(f32[2048]{0:T(1024)} %param.11) | copy-start | bytes 24580
  104.1 6.9 %copy-start.6 = (s32[1,384,6]{1,0,2:T(1,128)S(1)}, s32[1,384,6]{1,0,2:T(1,128)}, u32[]{:S(2)}) copy-start(s32[1,384,6]{1,0,2:T(1,128)} %param.13) | copy-start | bytes 27652
  109.1 1.0 copy-start.2
  326.5 5.9 %copy-start.4 = (bf16[384,2048]{1,0:T(8,128)(2,1)S(1)}, bf16[384,2048]{1,0:T(8,128)(2,1)}, u32[]{:S(2)}) copy-start(bf16[384,2048]{1,0:T(8,128)(2,1)} %all-gather.5.cloned.1.call-done) | copy-start | bytes 4718596
  326.5 5.9 %copy-start.5 = (bf16[2048,64]{0,1:T(8,128)(2,1)S(1)}, bf16[2048,64]{0,1:T(8,128)(2,1)}, u32[]{:S(2)}) copy-start(bf16[2048,64]{0,1:T(8,128)(2,1)} %param.12) | copy-start | bytes 786436
  326.5 182.3 %all-to-all-start.3 = ((bf16[32,2,48,2048]{3,2,1,0:T(8,128)(2,1)}), bf16[32,2,48,2048]{3,2,1,0:T(8,128)(2,1)}, u32[]{:S(2)}, u32[]{:S(2)}) async-start(bf16[32,2,48,2048]{3,2,1,0:T(8,128)(2,1)} %copy.128), calls=%async_computation.3 | async-start | bytes 25165824 | tf_op jit(solution)/shard_map/all_to_all | solution.py:116
  331.7 242.5 %reduce-scatter.2.cloned.1.call-start = ((), (), s32[]{:S(2)}) async-start(), calls=%async_computation.7 | async-start | bytes 1966080 | tf_op jit(solution)/shard_map/reduce_scatter | solution.py:118
  508.9 11.0 %copy-start.3 = (f32[384,3072]{1,0:T(8,128)S(1)}, f32[384,3072]{1,0:T(8,128)}, u32[]{:S(2)}) copy-start(f32[384,3072]{1,0:T(8,128)} %select_reduce_fusion) | copy-start | bytes 14155780
  519.9 56.3 %copy-start.1 = (bf16[2,352,2048]{2,1,0:T(8,128)(2,1)S(1)}, bf16[2,352,2048]{2,1,0:T(8,128)(2,1)}, u32[]{:S(2)}) copy-start(bf16[2,352,2048]{2,1,0:T(8,128)(2,1)} %param.15) | copy-start | bytes 8650756
Sparse Core Ops, SparseCore 0:
  9.0 95.0 all-gather.2
  111.1 27.2 all-gather.4
  529.9 44.2 reduce-scatter.1
where the time goes:
time: 583 us
  waiting for transfers between devices  263 us (45%)
  blocking collectives  190 us (33%)
  matrix products  68 us (12%)
  local copies, waits for them, and re-layouts  23.2 us (4%)
  other arithmetic  18.9 us (3%)
  between operations  13.3 us (2%)
    all_to_all x1, waiting for transfers between devices, on_device(): lax.all_to_all(partial_out, 'exp', split_axis=0, concat_axis=0, tiled=True)  167 us
    all_to_all x1, blocking collectives, on_device(): lax.all_to_all(outgoing, 'exp', split_axis=0, concat_axis=0, tiled=True)  148 us
    reduce_scatter x1, waiting for transfers between devices, on_device(): lax.psum_scatter(combine_rows(out_table, slot_index, gate_vals).astype(jn...  44.4 us
    all_gather x1, waiting for transfers between devices, on_device(): lax.all_gather(w_out, 'seq', axis=0, tiled=True)  30.5 us
    all_to_all x1, blocking collectives, on_device(): lax.all_to_all(packed, 'seq', split_axis=2, concat_axis=0, tiled=True)  27.4 us
    all_gather x1, waiting for transfers between devices, on_device(): gathered = lax.all_gather(normed, 'seq', axis=0, tiled=True)  20.6 us
    dot_general x1, matrix products, expert_part(): jnp.einsum('aend,edgf->aengf', received, w_gate_up, preferred_element_typ...  16 us
    all_to_all x1, blocking collectives, on_device(): lax.all_to_all(attended.reshape(seq_length, 1, local_width), 'seq', split...  15.5 us
  transfers between devices with their start and end apart: 4, of which 4 were waited for; matrix products, arithmetic and copies ran while one was open for 7% of the time, Pallas kernels for 0%

commit v1 on v0

--- a/solution.py
+++ b/solution.py
@@ -87,8 +87,19 @@
         attend_block, queries.reshape(seq_length // query_block, query_block, head_local, HD)
     )
     attended = attended.reshape(seq_length, local_width)
-    back = lax.all_to_all(
-        attended.reshape(seq_length, 1, local_width), "seq", split_axis=0, concat_axis=1, tiled=True
+    back = jnp.concatenate(
+        lax.all_to_all(
+            jnp.stack(
+                jnp.split(
+                    attended.reshape(seq_length, 1, local_width), lax.axis_size("seq"), axis=0
+                ),
+                axis=0,
+            ),
+            split_axis=0,
+            concat_axis=0,
+            axis_name="seq",
+        ),
+        axis=1,
     )
     point_rows = back.reshape(row_count, model_width)
     projected = jnp.dot(

time: 583 us -> 583 us (level)
  waiting for transfers between devices: 263 us -> 271 us
    all_gather x1, waiting for transfers between devices: 30.5 us -> 38 us  [on_device(): lax.all_gather(w_out, 'seq', axis=0, tiled=True)]
  transfers between devices with their start and end apart: 4 -> 4, of which waited for: 4 -> 4; matrix products, arithmetic and copies ran while one was open for 7% -> 6% of each run, Pallas kernels for 0% -> 0%
where the time goes in v1:
time: 583 us
  waiting for transfers between devices  271 us (46%)
  blocking collectives  189 us (32%)
  matrix products  68 us (12%)
  local copies, waits for them, and re-layouts  18.1 us (3%)
  other arithmetic  17.4 us (3%)
  between operations  13.4 us (2%)
    all_to_all x1, waiting for transfers between devices, on_device(): lax.all_to_all(partial_out, 'exp', split_axis=0, concat_axis=0, tiled=True)  167 us
    all_to_all x1, blocking collectives, on_device(): lax.all_to_all(outgoing, 'exp', split_axis=0, concat_axis=0, tiled=True)  148 us
    reduce_scatter x1, waiting for transfers between devices, on_device(): lax.psum_scatter(combine_rows(out_table, slot_index, gate_vals).astype(jn...  44.4 us
    all_gather x1, waiting for transfers between devices, on_device(): lax.all_gather(w_out, 'seq', axis=0, tiled=True)  38 us
    all_to_all x1, blocking collectives, on_device(): lax.all_to_all(packed, 'seq', split_axis=2, concat_axis=0, tiled=True)  27.4 us
    all_gather x1, waiting for transfers between devices, on_device(): gathered = lax.all_gather(normed, 'seq', axis=0, tiled=True)  20.6 us
    dot_general x1, matrix products, expert_part(): jnp.einsum('aend,edgf->aengf', received, w_gate_up, preferred_element_typ...  16 us
    all_to_all x1, blocking collectives, on_device(): lax.all_to_all(jnp.stack(jnp.split(attended.reshape(seq_length, 1, local_...  14.5 us
  transfers between devices with their start and end apart: 4, of which 4 were waited for; matrix products, arithmetic and copies ran while one was open for 6% of the time, Pallas kernels for 0%

profile of v1, /device:TPU:0, one launch (start us, length us, event | category | flops | bytes accessed | tf_op | source)
XLA Modules:
  0.0 582.8 jit_solution(17991028955438366877)
XLA Ops:
  7.3 2.9 reshape.144
  10.2 1.5 copy.130
  11.7 27.4 %all_to_all.33 = bf16[96,3,4,512]{3,0,1,2:T(8,128)(2,1)S(1)} all-to-all(bf16[96,3,4,512]{3,0,1,2:T(8,128)(2,1)S(1)} %copy.130), channel_id=1, replica_groups=mesh['seq'=4,'exp'=32] {'seq'}, dimensions={2} | all-to-all | bytes 2359296 | tf_op jit(solution)/shard_map/all_to_all | solution.py:70
  40.2 1.9 copy.132
  42.2 1.9 copy.133
  45.0 3.5 fusion.51
  48.5 2.3 fusion.28
  51.3 14.5 %all_to_all.34 = bf16[4,96,1,512]{3,1,2,0:T(8,128)(2,1)S(1)} all-to-all(bf16[4,96,1,512]{3,1,2,0:T(8,128)(2,1)S(1)} %pad_maximum_fusion), channel_id=1, replica_groups=mesh['seq'=4,'exp'=32] {'seq'}, dimensions={0} | all-to-all | bytes 786432 | tf_op jit(solution)/shard_map/all_to_all | solution.py:91
  66.1 38.0 %all-gather.3.cloned.1.call-done = bf16[2048,2048]{1,0:T(8,128)(2,1)} async-done(((bf16[512,2048]{1,0:T(8,128)(2,1)}), bf16[2048,2048]{1,0:T(8,128)(2,1)}) %all-gather.3.cloned.1.call-update) | async-done | bytes 8388624 | tf_op jit(solution)/shard_map/all_gather | solution.py:107
  104.1 5.0 multiply_reduce_fusion.1
  112.2 5.6 fusion.2
  117.8 20.6 %all-gather.5.cloned.1.call-done = bf16[384,2048]{1,0:T(8,128)(2,1)} async-done(((bf16[96,2048]{1,0:T(8,128)(2,1)}), bf16[384,2048]{1,0:T(8,128)(2,1)}) %all-gather.5.cloned.1.call-update) | async-done | bytes 1572880 | tf_op jit(solution)/shard_map/all_gather | solution.py:115
  138.4 8.7 %convolution_convert_fusion = bf16[3072,2048]{1,0:T(8,128)(2,1)S(1)} fusion(bf16[3072,384]{1,0:T(8,128)(2,1)} %fusion.2, bf16[384,2048]{1,0:T(8,128)(2,1)} %all-gather.5.cloned.1.call-done), kind=kOutput, calls=%fused_computation.9 | convolution fusion | flops 4838129664 | bytes 16515072 | tf_op jit(solution)/shard_map/dot_general | solution.py:45
  147.1 147.5 %all_to_all.35 = bf16[32,2,48,2048]{3,2,1,0:T(8,128)(2,1)} all-to-all(bf16[32,2,48,2048]{3,2,1,0:T(8,128)(2,1)S(1)} %bitcast.96), channel_id=1, replica_groups=mesh['seq'=4,'exp'=32] {'exp'}, dimensions={0} | all-to-all | bytes 25165824 | tf_op jit(solution)/shard_map/all_to_all | solution.py:125
  294.6 16.0 %fusion.8 = f32[32,2,48,2,352]{4,2,3,0,1:T(8,128)} fusion(bf16[2,2048,2,352]{1,3,2,0:T(8,128)(2,1)} %param.14, bf16[32,2,48,2048]{3,2,1,0:T(8,128)(2,1)} %all_to_all.35), kind=kOutput, calls=%fused_computation.16 | convolution fusion | flops 8858370048 | bytes 27000832 | tf_op jit(solution)/shard_map/aend,edgf->aengf/dot_general | solution.py:37
  310.6 10.7 %convert_bitcast_fusion = bf16[32,2,48,2048]{3,2,0,1:T(8,128)(2,1)S(1)} fusion(bf16[2,352,2048]{2,1,0:T(8,128)(2,1)S(1)} %copy-done, f32[32,2,48,2,352]{4,2,3,0,1:T(8,128)} %fusion.8), kind=kOutput, calls=%fused_computation.8 | convolution fusion | flops 4441964544 | bytes 24117248 | tf_op jit(solution)/shard_map/aenf,efd->aend/dot_general | solution.py:39
  321.3 5.2 copy.151
  326.5 5.2 all-to-all-start.3
  333.2 8.6 %select_reduce_fusion = f32[384,3072]{1,0:T(8,128)} fusion(f32[384,6]{0,1:T(8,128)S(1)} %multiply_divide_fusion, s32[384,6]{0,1:T(8,128)S(1)} %copy.146), kind=kLoop, calls=%fused_computation.2 | loop fusion | flops 20054016 | bytes 4737024 | tf_op jit(solution)/shard_map/reduce_sum | solution.py:50
  341.7 167.1 %all-to-all-done.3 = bf16[32,2,48,2048]{3,2,1,0:T(8,128)(2,1)} async-done(((bf16[32,2,48,2048]{3,2,1,0:T(8,128)(2,1)}), bf16[32,2,48,2048]{3,2,1,0:T(8,128)(2,1)}, u32[]{:S(2)}, u32[]{:S(2)}) %all-to-all-start.3) | async-done | bytes 12582944 | tf_op jit(solution)/shard_map/all_to_all | solution.py:127
  508.9 11.0 %fusion.33 = f32[384,2048]{1,0:T(8,128)S(1)} fusion(bf16[3072,2048]{1,0:T(8,128)(2,1)} %bitcast.25, f32[384,3072]{1,0:T(8,128)} %select_reduce_fusion), kind=kOutput, calls=%fused_computation.34 | convolution fusion | flops 4833017856 | bytes 20447232 | tf_op jit(solution)/shard_map/dot_general | solution.py:56
  519.9 9.8 %add_convert_fusion = bf16[384,2048]{1,0:T(8,128)(2,1)} fusion(f32[384,2048]{1,0:T(8,128)S(1)} %fusion.33, bf16[3072,2048]{1,0:T(8,128)(2,1)} %bitcast.25, f32[384,3072]{1,0:T(8,128)S(1)} %copy-done.3), kind=kOutput, calls=%fused_computation.17 | convolution fusion | flops 4838129664 | bytes 22020096 | tf_op jit(solution)/shard_map/dot_general | solution.py:56
  529.7 44.4 %reduce-scatter.2.cloned.1.call-done = bf16[96,2048]{1,0:T(8,128)(2,1)} async-done(((bf16[384,2048]{1,0:T(8,128)(2,1)}), bf16[96,2048]{1,0:T(8,128)(2,1)}) %reduce-scatter.2.cloned.1.call-update) | async-done | bytes 393232 | tf_op jit(solution)/shard_map/reduce_scatter | solution.py:129
  574.2 2.1 fusion.37
  (56 shorter events, 8.0 us)
Async XLA Ops:
  6.5 304.1 %copy-start = (bf16[2,352,2048]{2,1,0:T(8,128)(2,1)S(1)}, bf16[2,352,2048]{2,1,0:T(8,128)(2,1)}, u32[]{:S(2)}) copy-start(bf16[2,352,2048]{2,1,0:T(8,128)(2,1)} %param.15) | copy-start | bytes 8650756
  6.5 97.6 %all-gather.3.cloned.1.call-start = ((), (), s32[]{:S(2)}) async-start(), calls=%async_computation.5 | async-start | bytes 10485760 | tf_op jit(solution)/shard_map/all_gather | solution.py:107
  7.3 131.1 %all-gather.5.cloned.1.call-start = ((), (), s32[]{:S(2)}) async-start(), calls=%async_computation.6 | async-start | bytes 1966080 | tf_op jit(solution)/shard_map/all_gather | solution.py:115
  104.1 6.0 %copy-start.7 = (f32[2048]{0:T(1024)S(1)}, f32[2048]{0:T(1024)}, u32[]{:S(2)}) copy-start(f32[2048]{0:T(1024)} %param.11) | copy-start | bytes 24580
  104.1 6.9 %copy-start.6 = (s32[1,384,6]{1,0,2:T(1,128)S(1)}, s32[1,384,6]{1,0,2:T(1,128)}, u32[]{:S(2)}) copy-start(s32[1,384,6]{1,0,2:T(1,128)} %param.13) | copy-start | bytes 27652
  109.1 1.0 copy-start.2
  326.5 5.9 %copy-start.4 = (bf16[384,2048]{1,0:T(8,128)(2,1)S(1)}, bf16[384,2048]{1,0:T(8,128)(2,1)}, u32[]{:S(2)}) copy-start(bf16[384,2048]{1,0:T(8,128)(2,1)} %all-gather.5.cloned.1.call-done) | copy-start | bytes 4718596
  326.5 5.9 %copy-start.5 = (bf16[2048,64]{0,1:T(8,128)(2,1)S(1)}, bf16[2048,64]{0,1:T(8,128)(2,1)}, u32[]{:S(2)}) copy-start(bf16[2048,64]{0,1:T(8,128)(2,1)} %param.12) | copy-start | bytes 786436
  326.5 182.3 %all-to-all-start.3 = ((bf16[32,2,48,2048]{3,2,1,0:T(8,128)(2,1)}), bf16[32,2,48,2048]{3,2,1,0:T(8,128)(2,1)}, u32[]{:S(2)}, u32[]{:S(2)}) async-start(bf16[32,2,48,2048]{3,2,1,0:T(8,128)(2,1)} %copy.151), calls=%async_computation.3 | async-start | bytes 25165824 | tf_op jit(solution)/shard_map/all_to_all | solution.py:127
  331.7 242.5 %reduce-scatter.2.cloned.1.call-start = ((), (), s32[]{:S(2)}) async-start(), calls=%async_computation.7 | async-start | bytes 1966080 | tf_op jit(solution)/shard_map/reduce_scatter | solution.py:129
  508.9 11.0 %copy-start.3 = (f32[384,3072]{1,0:T(8,128)S(1)}, f32[384,3072]{1,0:T(8,128)}, u32[]{:S(2)}) copy-start(f32[384,3072]{1,0:T(8,128)} %select_reduce_fusion) | copy-start | bytes 14155780
  519.9 56.3 %copy-start.1 = (bf16[2,352,2048]{2,1,0:T(8,128)(2,1)S(1)}, bf16[2,352,2048]{2,1,0:T(8,128)(2,1)}, u32[]{:S(2)}) copy-start(bf16[2,352,2048]{2,1,0:T(8,128)(2,1)} %param.15) | copy-start | bytes 8650756
Sparse Core Ops, SparseCore 0:
  9.0 95.0 all-gather.2
  111.1 27.2 all-gather.4
  529.9 44.2 reduce-scatter.1
